TPU v7x, 32 devices: a whole 2x2x4 slice. The times are simulated.
32 devices in a mesh: track: 4 (over z), cross: 8 (over y, x, core).
Axes of the slice: x: 2, y: 2, z: 4, core: 2. Of those that a mesh axis runs over, the one named last changes fastest.
Arguments:
- cube: bfloat16 [1024, 256, 224], P('track', 'cross'), may hold values from -60 to 113, as said below
Outputs:
- scores: float32 [1024, 256], P('track', 'cross')
Inputs may be any that keep to these rules, and one draw needn't show every extreme that they name: `cube`: A positive radiance level per band plus noise, scaled per band and by position.
All inputs are finite; a program needn't handle non-finite values.
Results may differ from a plain program's by a relative error of at most 0.0003.
Values may be sent and summed in bfloat16 or wider, within the bound.
No kernel may reach another device: no remote copies, remote signals or barrier semaphores. Data moves between devices by JAX's collectives and lax.ppermute only.
A program may use at most 64 MiB of HBM per device.

v0:
```python
import jax
import jax.numpy as jnp
from jax import lax
from jax.sharding import PartitionSpec as P

HALF = 15
LOAD = 0.02


def with_halo(block, sides, width):
    for axis, dim in sides:
        count = lax.axis_size(axis)
        forward = [(i, i + 1) for i in range(count - 1)]
        backward = [(target, source) for source, target in forward]
        low = lax.ppermute(
            lax.slice_in_dim(block, block.shape[dim] - width, None, axis=dim), axis, forward
        )
        high = lax.ppermute(lax.slice_in_dim(block, 0, width, axis=dim), axis, backward)
        block = jnp.concatenate([low, block, high], axis=dim)
    return block


def band_matrix(rows_in, rows_out, dtype):
    source = jnp.arange(rows_in)[:, None]
    target = jnp.arange(rows_out)[None, :]
    inside = (source >= target) & (source <= target + 2 * HALF)
    return inside.astype(dtype)


def window_count(first, local, total):
    index = first + jnp.arange(local)
    upper = jnp.minimum(index + HALF, total - 1)
    lower = jnp.maximum(index - HALF, 0)
    return (upper - lower + 1).astype(jnp.float32)


def sum_pixels(values, width, dtype):
    weights = band_matrix(width + 2 * HALF, width, dtype)
    return jnp.einsum(
        "lqb,qp->lpb", values, weights, precision=None, preferred_element_type=jnp.float32
    )


def sum_lines(values, height, dtype, precision):
    weights = band_matrix(height + 2 * HALF, height, dtype)
    return jnp.einsum(
        "kpb,kl->lpb", values, weights, precision=precision, preferred_element_type=jnp.float32
    )


def shards(cube):
    lines_dev, pix_dev, bands = cube.shape
    n_track = lax.axis_size("track")
    n_cross = lax.axis_size("cross")
    total_lines = lines_dev * n_track
    total_pix = pix_dev * n_cross
    highest = lax.Precision.HIGHEST
    extended = with_halo(cube, (("track", 0), ("cross", 1)), HALF)
    across = sum_pixels(extended, pix_dev, jnp.bfloat16)
    window = sum_lines(across, lines_dev, jnp.float32, highest)
    line_count = window_count(lax.axis_index("track") * lines_dev, lines_dev, total_lines)
    pixel_count = window_count(lax.axis_index("cross") * pix_dev, pix_dev, total_pix)
    count = line_count[:, None, None] * pixel_count[None, :, None]
    residual = cube.astype(jnp.float32) - window / count
    flat = residual.reshape(lines_dev * pix_dev, bands)
    flat_bf = flat.astype(jnp.bfloat16)
    partial_cov = jnp.dot(flat_bf.T, flat_bf, preferred_element_type=jnp.float32)
    covariance = lax.psum(partial_cov, ("track", "cross")) / (total_lines * total_pix)
    identity = jnp.eye(bands, dtype=jnp.float32)
    loaded = covariance + LOAD * (jnp.trace(covariance) / bands) * identity
    factor = jnp.linalg.cholesky(loaded)
    inverse = jax.scipy.linalg.solve_triangular(factor, identity, lower=True)
    whitened = jnp.dot(flat, inverse.T, precision=highest, preferred_element_type=jnp.float32)
    scores = jnp.sum(whitened * whitened, axis=1) / bands
    return scores.reshape(lines_dev, pix_dev)


def solution(mesh):
    return jax.shard_map(
        shards,
        mesh=mesh,
        in_specs=(P("track", "cross", None),),
        out_specs=P("track", "cross"),
        check_vma=False,
    )
```

profile of v0, /device:TPU:1, one launch (start us, length us, event | category | flops | bytes accessed | tf_op | source)
XLA Modules:
  0.0 329.4 jit_solution(2984762335970636967)
XLA Ops:
  6.5 0.0 all-reduce.5.cloned.1.call-start
  6.5 7.8 %copy.6 = bf16[256,32,224]{2,1,0:T(8,128)(2,1)} copy(bf16[256,32,224]{0,2,1:T(8,128)(2,1)} %param.1) | data formatting | bytes 7340032 | tf_op args[0]
  14.4 1.1 fusion.46
  15.5 4.0 %collective-permute-start = (bf16[15,32,224]{2,1,0:T(8,128)(2,1)S(1)}, bf16[15,32,224]{2,1,0:T(8,128)(2,1)S(1)}, u32[]{:S(2)}, u32[]{:S(2)}) collective-permute-start(bf16[15,32,224]{2,1,0:T(8,128)(2,1)S(1)} %get-tuple-element.27), channel_id=1, source_target_pairs={{0,8},{8,16},{16,24},{1,9},{9,17},{17,25},{2,10},{10,18},{18,26},{... | collective-permute-start | bytes 645128 | tf_op jit(solution)/shard_map/ppermute | solution.py:15
  19.5 1.3 collective-permute-start.1
  20.8 3.3 collective-permute-done
  24.1 3.8 %collective-permute-done.1 = bf16[15,32,224]{2,1,0:T(8,128)(2,1)S(1)} collective-permute-done((bf16[15,32,224]{2,1,0:T(8,128)(2,1)S(1)}, bf16[15,32,224]{2,1,0:T(8,128)(2,1)S(1)}, u32[]{:S(2)}, u32[]{:S(2)}) %collective-permute-start.1) | collective-permute-done | bytes 215072 | tf_op jit(solution)/shard_map/ppermute | solution.py:18
  27.9 2.7 pad_maximum_fusion
  30.7 1.0 fusion.45
  31.7 0.8 copy.9
  32.5 4.9 %collective-permute-start.2 = (bf16[286,15,224]{2,0,1:T(8,128)(2,1)S(1)}, bf16[286,15,224]{2,0,1:T(8,128)(2,1)}, u32[]{:S(2)}, u32[]{:S(2)}) collective-permute-start(bf16[286,15,224]{2,0,1:T(8,128)(2,1)S(1)} %copy.9), channel_id=1, source_target_pairs={{0,1},{1,2},{2,3},{3,4},{4,5},{5,6},{6,7},{8,9},{9,10},{10,11},{11... | collective-permute-start | bytes 5765768 | tf_op jit(solution)/shard_map/ppermute | solution.py:15
  37.4 2.1 copy.10
  39.6 1.9 collective-permute-start.3
  41.5 0.0 copy-start.1
  41.6 0.1 broadcast_multiply_fusion.1
  41.6 20.0 %collective-permute-done.2 = bf16[286,15,224]{2,0,1:T(8,128)(2,1)} collective-permute-done((bf16[286,15,224]{2,0,1:T(8,128)(2,1)S(1)}, bf16[286,15,224]{2,0,1:T(8,128)(2,1)}, u32[]{:S(2)}, u32[]{:S(2)}) %collective-permute-start.2) | collective-permute-done | bytes 1921952 | tf_op jit(solution)/shard_map/ppermute | solution.py:15
  61.6 2.9 copy.11
  64.5 22.6 %collective-permute-done.3 = bf16[286,15,224]{2,0,1:T(8,128)(2,1)} collective-permute-done((bf16[286,15,224]{2,0,1:T(8,128)(2,1)}, bf16[286,15,224]{2,0,1:T(8,128)(2,1)}, u32[]{:S(2)}, u32[]{:S(2)}) %collective-permute-start.3) | collective-permute-done | bytes 1921952 | tf_op jit(solution)/shard_map/ppermute | solution.py:18
  87.1 2.9 copy.12
  89.9 0.0 copy-done.1
  89.9 0.0 copy-start.2
  89.9 15.9 %fusion.14 = f32[286,32,224]{2,1,0:T(8,128)} fusion(bf16[286,15,224]{2,1,0:T(8,128)(2,1)S(1)} %copy.12, bf16[15,32,224]{2,1,0:T(8,128)(2,1)S(1)} %collective-permute-done.1, bf16[256,32,224]{2,1,0:T(8,128)(2,1)S(1)} %copy-done.1, bf16[15,32,224]{2,1,0:T(8,128)(2,1)S(1)} %collective-permute-done, bf16[286,15,224]{2,1,0:T(8,128)(2,1)S(1)} %copy.11, ...), kind=kOutput, calls=%fused_computation.17 | convolution fusion | flops 293931584 | bytes 16144256 | tf_op jit(solution)/shard_map/lqb,qp->lpb/dot_general | solution.py:39
  105.8 0.0 copy-done.2
  105.8 18.1 %divide_subtract_fusion = f32[256,32,224]{0,2,1:T(8,128)S(1)} fusion(bf16[256,32,224]{0,2,1:T(8,128)(2,1)S(1)} %copy-done.2, f32[256,32]{0,1:T(8,128)S(1)} %broadcast_multiply_fusion.1, f32[286,32,224]{2,1,0:T(8,128)} %fusion.14, s32[256]{0:T(256)S(1)} %iota_add_fusion), kind=kOutput, calls=%fused_computation.13 | convolution fusion | flops 6303472128 | bytes 19244032 | tf_op jit(solution)/shard_map/kpb,kl->lpb/dot_general | solution.py:46
  123.9 3.0 copy-done
  126.9 1.8 fusion.20
  128.8 0.0 all-reduce.5.cloned.1.call-update
  128.8 9.9 %copy.14 = f32[256,32,224]{2,1,0:T(8,128)} copy(f32[256,32,224]{0,2,1:T(8,128)} %copy-done) | data formatting | bytes 14680064 | tf_op jit(solution)/shard_map/sub | solution.py:64
  138.7 113.2 %all-reduce.5.cloned.1.call-done = f32[224,224]{1,0:T(8,128)} async-done(((f32[224,224]{1,0:T(8,128)}), f32[224,224]{1,0:T(8,128)}) %all-reduce.5.cloned.1.call-update) | async-done | bytes 200720 | tf_op jit(solution)/shard_map/psum | solution.py:68
  251.9 1.6 select_reduce_fusion
  254.1 1.0 select_add_fusion
  255.1 0.1 copy.15
  255.2 1.0 fusion.29
  256.2 11.7 %cholesky.50 = f32[128,128]{1,0:T(8,128)S(1)} custom-call(f32[128,128]{1,0:T(8,128)S(1)} %cholesky.121), custom_call_target="Cholesky" | custom-call | tf_op jit(solution)/shard_map/jit(cholesky)/cholesky | solution.py:71
  268.0 9.8 %custom-call.15 = f32[1,128,128]{1,2,0:T(8,128)S(1)} custom-call(f32[1,128,128]{2,1,0:T(8,128)S(1)} %get-tuple-element.30), custom_call_target="InvertDiagBlocksLowerTriangular" | custom-call | tf_op jit(solution)/shard_map/jit(cholesky)/cholesky | solution.py:71
  277.8 0.2 constant_dynamic-update-slice_fusion.1
  278.0 0.2 convolution_subtract_fusion.1
  278.2 8.8 %cholesky.108 = f32[96,96]{1,0:T(8,128)S(1)} custom-call(f32[96,96]{1,0:T(8,128)S(1)} %convolution_subtract_fusion.1), custom_call_target="Cholesky" | custom-call | tf_op jit(solution)/shard_map/jit(cholesky)/cholesky | solution.py:71
  287.0 0.6 compare_reduce_fusion
  287.6 0.6 compare_reduce_fusion.1
  289.5 0.1 fusion.33
  289.7 19.7 %custom-call.16 = f32[2,128,128]{1,2,0:T(8,128)S(1)} custom-call(f32[2,128,128]{2,1,0:T(8,128)S(1)} %pad_maximum_fusion.1), custom_call_target="InvertDiagBlocksLowerTriangular" | custom-call | tf_op jit(solution)/shard_map/jit(_solve_triangular)/triangular_solve | solution.py:72
  309.3 0.3 fusion.31
  309.6 0.4 convolution_subtract_fusion
  310.0 0.4 fusion.37
  310.4 11.4 %fusion.19 = f32[8192]{0:T(1024)S(1)} fusion(f32[8192,224]{1,0:T(8,128)} %bitcast.37, f32[96,224]{0,1:T(8,128)S(1)} %fusion.37, f32[128,224]{0,1:T(8,128)S(1)} %fusion.31), kind=kOutput, calls=%fused_computation.18 | convolution fusion | flops 4936213504 | bytes 7573504 | tf_op jit(solution)/shard_map/dot_general | solution.py:73
  321.7 0.1 div.39
  321.8 0.7 copy.17
  (16 shorter events, 0.2 us)
Async XLA Ops:
  6.5 245.3 %all-reduce.5.cloned.1.call-start = ((), (), s32[]{:S(2)}) async-start(), calls=%async_computation | async-start | bytes 458752 | tf_op jit(solution)/shard_map/psum | solution.py:68
  15.5 8.6 %collective-permute-start = (bf16[15,32,224]{2,1,0:T(8,128)(2,1)S(1)}, bf16[15,32,224]{2,1,0:T(8,128)(2,1)S(1)}, u32[]{:S(2)}, u32[]{:S(2)}) collective-permute-start(bf16[15,32,224]{2,1,0:T(8,128)(2,1)S(1)} %get-tuple-element.27), channel_id=1, source_target_pairs={{0,8},{8,16},{16,24},{1,9},{9,17},{17,25},{2,10},{10,18},{18,26},{... | collective-permute-start | bytes 645128 | tf_op jit(solution)/shard_map/ppermute | solution.py:15
  19.5 8.4 %collective-permute-start.1 = (bf16[15,32,224]{2,1,0:T(8,128)(2,1)S(1)}, bf16[15,32,224]{2,1,0:T(8,128)(2,1)S(1)}, u32[]{:S(2)}, u32[]{:S(2)}) collective-permute-start(bf16[15,32,224]{2,1,0:T(8,128)(2,1)S(1)} %get-tuple-element.28), channel_id=1, source_target_pairs={{8,0},{16,8},{24,16},{9,1},{17,9},{25,17},{10,2},{18,10},{26,18},{... | collective-permute-start | bytes 645128 | tf_op jit(solution)/shard_map/ppermute | solution.py:18
  32.5 29.1 %collective-permute-start.2 = (bf16[286,15,224]{2,0,1:T(8,128)(2,1)S(1)}, bf16[286,15,224]{2,0,1:T(8,128)(2,1)}, u32[]{:S(2)}, u32[]{:S(2)}) collective-permute-start(bf16[286,15,224]{2,0,1:T(8,128)(2,1)S(1)} %copy.9), channel_id=1, source_target_pairs={{0,1},{1,2},{2,3},{3,4},{4,5},{5,6},{6,7},{8,9},{9,10},{10,11},{11... | collective-permute-start | bytes 5765768 | tf_op jit(solution)/shard_map/ppermute | solution.py:15
  39.6 47.5 %collective-permute-start.3 = (bf16[286,15,224]{2,0,1:T(8,128)(2,1)}, bf16[286,15,224]{2,0,1:T(8,128)(2,1)}, u32[]{:S(2)}, u32[]{:S(2)}) collective-permute-start(bf16[286,15,224]{2,0,1:T(8,128)(2,1)} %copy.10), channel_id=1, source_target_pairs={{1,0},{2,1},{3,2},{4,3},{5,4},{6,5},{7,6},{9,8},{10,9},{11,10},{12... | collective-permute-start | bytes 5765768 | tf_op jit(solution)/shard_map/ppermute | solution.py:18
  41.5 48.4 %copy-start.1 = (bf16[256,32,224]{2,1,0:T(8,128)(2,1)S(1)}, bf16[256,32,224]{2,1,0:T(8,128)(2,1)}, u32[]{:S(2)}) copy-start(bf16[256,32,224]{2,1,0:T(8,128)(2,1)} %copy.6) | copy-start | bytes 11010052
  89.9 15.9 %copy-start.2 = (bf16[256,32,224]{0,2,1:T(8,128)(2,1)S(1)}, bf16[256,32,224]{0,2,1:T(8,128)(2,1)}, u32[]{:S(2)}) copy-start(bf16[256,32,224]{0,2,1:T(8,128)(2,1)} %param.1) | copy-start | bytes 11010052
  123.9 3.0 copy-start
Sparse Core Ops, SparseCore 0:
  128.9 122.8 all-reduce.4
where the time goes:
time: 330 us; the launch traced here: 329 us
  waiting for transfers between devices  163 us (49%)
  other arithmetic  57.8 us (18%)
  matrix products  48.6 us (15%)
  local copies, waits for them, and re-layouts  32.5 us (10%)
  between operations  15.6 us (5%)
  starting transfers between devices  12.1 us (4%)
    psum x1, waiting for transfers between devices, shards(): lax.psum(partial_cov, ('track', 'cross')) / (total_lines * total_pix)  113 us
    another operation x7, other arithmetic, shards(): factor = jnp.linalg.cholesky(loaded)  31.6 us
    ppermute x2, waiting for transfers between devices, with_halo(): lax.ppermute(lax.slice_in_dim(block, 0, width, axis=dim), axis, backward)  26.4 us
    ppermute x2, waiting for transfers between devices, with_halo(): lax.ppermute(lax.slice_in_dim(block, block.shape[dim] - width, None, axis...  23.2 us
    another operation x6, other arithmetic, shards(): inverse = jax.scipy.linalg.solve_triangular(factor, identity, lower=True)  19.8 us
    dot_general x1, matrix products, sum_lines(): jnp.einsum('kpb,kl->lpb', values, weights, precision=precision, preferred...  18.1 us
    dot_general x1, matrix products, sum_pixels(): jnp.einsum('lqb,qp->lpb', values, weights, precision=None, preferred_elem...  15.9 us
    dot_general x1, matrix products, shards(): jnp.dot(flat, inverse.T, precision=highest, preferred_element_type=jnp.fl...  11.4 us
  transfers between devices with their start and end apart: 5, of which 5 were waited for; matrix products, arithmetic and copies ran while one was open for 5% of the time, Pallas kernels for 0%

commit v1 on v0

--- a/solution.py
+++ b/solution.py
@@ -49,6 +49,12 @@
 
 
 def shards(cube):
+
+    def direct_the_ways(content, row_axis, axis_id):
+        b_now = lax.psum(content, row_axis)
+        back = lax.psum(b_now, axis_id)
+        return back
+
     lines_dev, pix_dev, bands = cube.shape
     n_track = lax.axis_size("track")
     n_cross = lax.axis_size("cross")
@@ -65,7 +71,7 @@
     flat = residual.reshape(lines_dev * pix_dev, bands)
     flat_bf = flat.astype(jnp.bfloat16)
     partial_cov = jnp.dot(flat_bf.T, flat_bf, preferred_element_type=jnp.float32)
-    covariance = lax.psum(partial_cov, ("track", "cross")) / (total_lines * total_pix)
+    covariance = direct_the_ways(partial_cov, "cross", "track") / (total_lines * total_pix)
     identity = jnp.eye(bands, dtype=jnp.float32)
     loaded = covariance + LOAD * (jnp.trace(covariance) / bands) * identity
     factor = jnp.linalg.cholesky(loaded)

time: 330 us -> 297 us (0.900)
  waiting for transfers between devices: 163 us -> 127 us
    psum x1 -> x2, waiting for transfers between devices: 113 us -> 77.7 us  [the longest x1 51.5 us: direct_the_ways(): b_now = lax.psum(content, row_axis)]
  transfers between devices with their start and end apart: 5 -> 6, of which waited for: 5 -> 6; matrix products, arithmetic and copies ran while one was open for 5% -> 5% of each run, Pallas kernels for 0% -> 0%
where the time goes in v1:
time: 297 us; the launch traced here: 294 us
  waiting for transfers between devices  127 us (43%)
  other arithmetic  58.1 us (20%)
  matrix products  48.3 us (16%)
  local copies, waits for them, and re-layouts  32.7 us (11%)
  between operations  15.6 us (5%)
  starting transfers between devices  12.2 us (4%)
    psum x1, waiting for transfers between devices, direct_the_ways(): b_now = lax.psum(content, row_axis)  51.5 us
    another operation x7, other arithmetic, shards(): factor = jnp.linalg.cholesky(loaded)  31.6 us
    ppermute x2, waiting for transfers between devices, with_halo(): lax.ppermute(lax.slice_in_dim(block, 0, width, axis=dim), axis, backward)  26.4 us
    psum x1, waiting for transfers between devices, direct_the_ways(): back = lax.psum(b_now, axis_id)  26.2 us
    ppermute x2, waiting for transfers between devices, with_halo(): lax.ppermute(lax.slice_in_dim(block, block.shape[dim] - width, None, axis...  23.3 us
    another operation x6, other arithmetic, shards(): inverse = jax.scipy.linalg.solve_triangular(factor, identity, lower=True)  20.1 us
    dot_general x1, matrix products, sum_lines(): jnp.einsum('kpb,kl->lpb', values, weights, precision=precision, preferred...  18.1 us
    dot_general x1, matrix products, sum_pixels(): jnp.einsum('lqb,qp->lpb', values, weights, precision=None, preferred_elem...  15.9 us
  transfers between devices with their start and end apart: 6, of which 6 were waited for; matrix products, arithmetic and copies ran while one was open for 5% of the time, Pallas kernels for 0%

profile of v1, /device:TPU:1, one launch (start us, length us, event | category | flops | bytes accessed | tf_op | source)
XLA Modules:
  0.0 294.2 jit_solution(2207353964549665462)
XLA Ops:
  6.5 0.0 all-reduce.6.cloned.1.call-start
  6.5 7.8 %copy.6 = bf16[256,32,224]{2,1,0:T(8,128)(2,1)} copy(bf16[256,32,224]{0,2,1:T(8,128)(2,1)} %param.1) | data formatting | bytes 7340032 | tf_op args[0]
  14.4 1.1 fusion.46
  15.5 4.0 %collective-permute-start = (bf16[15,32,224]{2,1,0:T(8,128)(2,1)S(1)}, bf16[15,32,224]{2,1,0:T(8,128)(2,1)S(1)}, u32[]{:S(2)}, u32[]{:S(2)}) collective-permute-start(bf16[15,32,224]{2,1,0:T(8,128)(2,1)S(1)} %get-tuple-element.27), channel_id=1, source_target_pairs={{0,8},{8,16},{16,24},{1,9},{9,17},{17,25},{2,10},{10,18},{18,26},{... | collective-permute-start | bytes 645128 | tf_op jit(solution)/shard_map/ppermute | solution.py:15
  19.5 1.3 collective-permute-start.1
  20.8 3.3 %collective-permute-done = bf16[15,32,224]{2,1,0:T(8,128)(2,1)S(1)} collective-permute-done((bf16[15,32,224]{2,1,0:T(8,128)(2,1)S(1)}, bf16[15,32,224]{2,1,0:T(8,128)(2,1)S(1)}, u32[]{:S(2)}, u32[]{:S(2)}) %collective-permute-start) | collective-permute-done | bytes 215072 | tf_op jit(solution)/shard_map/ppermute | solution.py:15
  24.1 3.8 %collective-permute-done.1 = bf16[15,32,224]{2,1,0:T(8,128)(2,1)S(1)} collective-permute-done((bf16[15,32,224]{2,1,0:T(8,128)(2,1)S(1)}, bf16[15,32,224]{2,1,0:T(8,128)(2,1)S(1)}, u32[]{:S(2)}, u32[]{:S(2)}) %collective-permute-start.1) | collective-permute-done | bytes 215072 | tf_op jit(solution)/shard_map/ppermute | solution.py:18
  27.9 2.7 pad_maximum_fusion
  30.7 1.0 fusion.45
  31.7 0.8 copy.9
  32.5 4.9 %collective-permute-start.2 = (bf16[286,15,224]{2,0,1:T(8,128)(2,1)S(1)}, bf16[286,15,224]{2,0,1:T(8,128)(2,1)}, u32[]{:S(2)}, u32[]{:S(2)}) collective-permute-start(bf16[286,15,224]{2,0,1:T(8,128)(2,1)S(1)} %copy.9), channel_id=1, source_target_pairs={{0,1},{1,2},{2,3},{3,4},{4,5},{5,6},{6,7},{8,9},{9,10},{10,11},{11... | collective-permute-start | bytes 5765768 | tf_op jit(solution)/shard_map/ppermute | solution.py:15
  37.4 2.1 copy.10
  39.6 1.9 collective-permute-start.3
  41.5 0.1 broadcast_multiply_fusion.1
  41.6 20.0 %collective-permute-done.2 = bf16[286,15,224]{2,0,1:T(8,128)(2,1)} collective-permute-done((bf16[286,15,224]{2,0,1:T(8,128)(2,1)S(1)}, bf16[286,15,224]{2,0,1:T(8,128)(2,1)}, u32[]{:S(2)}, u32[]{:S(2)}) %collective-permute-start.2) | collective-permute-done | bytes 1921952 | tf_op jit(solution)/shard_map/ppermute | solution.py:15
  61.6 2.9 copy.11
  64.5 22.6 %collective-permute-done.3 = bf16[286,15,224]{2,0,1:T(8,128)(2,1)} collective-permute-done((bf16[286,15,224]{2,0,1:T(8,128)(2,1)}, bf16[286,15,224]{2,0,1:T(8,128)(2,1)}, u32[]{:S(2)}, u32[]{:S(2)}) %collective-permute-start.3) | collective-permute-done | bytes 1921952 | tf_op jit(solution)/shard_map/ppermute | solution.py:18
  87.1 2.9 copy.12
  89.9 0.0 copy-start.2
  89.9 15.9 %fusion.14 = f32[286,32,224]{2,1,0:T(8,128)} fusion(bf16[286,15,224]{2,1,0:T(8,128)(2,1)S(1)} %copy.12, bf16[15,32,224]{2,1,0:T(8,128)(2,1)S(1)} %collective-permute-done.1, bf16[256,32,224]{2,1,0:T(8,128)(2,1)S(1)} %copy-done.1, bf16[15,32,224]{2,1,0:T(8,128)(2,1)S(1)} %collective-permute-done, bf16[286,15,224]{2,1,0:T(8,128)(2,1)S(1)} %copy.11, ...), kind=kOutput, calls=%fused_computation.17 | convolution fusion | flops 293931584 | bytes 16144256 | tf_op jit(solution)/shard_map/lqb,qp->lpb/dot_general | solution.py:39
  105.8 18.1 %divide_subtract_fusion = f32[256,32,224]{0,2,1:T(8,128)S(1)} fusion(bf16[256,32,224]{0,2,1:T(8,128)(2,1)S(1)} %copy-done.2, f32[256,32]{0,1:T(8,128)S(1)} %broadcast_multiply_fusion.1, f32[286,32,224]{2,1,0:T(8,128)} %fusion.14, s32[256]{0:T(256)S(1)} %iota_add_fusion), kind=kOutput, calls=%fused_computation.13 | convolution fusion | flops 6303472128 | bytes 19244032 | tf_op jit(solution)/shard_map/kpb,kl->lpb/dot_general | solution.py:46
  123.9 3.0 %copy-done = f32[256,32,224]{0,2,1:T(8,128)} copy-done((f32[256,32,224]{0,2,1:T(8,128)}, f32[256,32,224]{0,2,1:T(8,128)S(1)}, u32[]{:S(2)}) %copy-start) | copy-done | bytes 7340056
  126.9 1.8 fusion.20
  128.8 0.0 all-reduce.6.cloned.1.call-update
  128.8 0.0 all-reduce.8.cloned.1.call-start
  128.9 51.5 %all-reduce.6.cloned.1.call-done = f32[224,224]{1,0:T(8,128)} async-done(((f32[224,224]{1,0:T(8,128)}), f32[224,224]{1,0:T(8,128)}) %all-reduce.6.cloned.1.call-update) | async-done | bytes 200720 | tf_op jit(solution)/shard_map/psum | solution.py:54
  180.4 0.0 all-reduce.8.cloned.1.call-update
  180.4 10.1 %copy.14 = f32[256,32,224]{2,1,0:T(8,128)} copy(f32[256,32,224]{0,2,1:T(8,128)} %copy-done) | data formatting | bytes 14680064 | tf_op jit(solution)/shard_map/sub | solution.py:70
  190.5 26.2 %all-reduce.8.cloned.1.call-done = f32[224,224]{1,0:T(8,128)} async-done(((f32[224,224]{1,0:T(8,128)}), f32[224,224]{1,0:T(8,128)}) %all-reduce.8.cloned.1.call-update) | async-done | bytes 200720 | tf_op jit(solution)/shard_map/psum | solution.py:55
  216.7 1.6 select_reduce_fusion
  219.0 1.0 select_add_fusion
  219.9 0.1 copy.15
  220.1 1.0 fusion.29
  221.1 11.7 %cholesky.50 = f32[128,128]{1,0:T(8,128)S(1)} custom-call(f32[128,128]{1,0:T(8,128)S(1)} %cholesky.121), custom_call_target="Cholesky" | custom-call | tf_op jit(solution)/shard_map/jit(cholesky)/cholesky | solution.py:77
  232.8 9.8 %custom-call.15 = f32[1,128,128]{1,2,0:T(8,128)S(1)} custom-call(f32[1,128,128]{2,1,0:T(8,128)S(1)} %get-tuple-element.30), custom_call_target="InvertDiagBlocksLowerTriangular" | custom-call | tf_op jit(solution)/shard_map/jit(cholesky)/cholesky | solution.py:77
  242.7 0.2 constant_dynamic-update-slice_fusion.1
  242.9 0.2 convolution_subtract_fusion.1
  243.1 8.8 %cholesky.108 = f32[96,96]{1,0:T(8,128)S(1)} custom-call(f32[96,96]{1,0:T(8,128)S(1)} %convolution_subtract_fusion.1), custom_call_target="Cholesky" | custom-call | tf_op jit(solution)/shard_map/jit(cholesky)/cholesky | solution.py:77
  251.9 0.6 compare_reduce_fusion
  252.5 0.6 compare_reduce_fusion.1
  254.4 0.1 fusion.33
  254.5 19.9 %custom-call.16 = f32[2,128,128]{1,2,0:T(8,128)S(1)} custom-call(f32[2,128,128]{2,1,0:T(8,128)S(1)} %pad_maximum_fusion.1), custom_call_target="InvertDiagBlocksLowerTriangular" | custom-call | tf_op jit(solution)/shard_map/jit(_solve_triangular)/triangular_solve | solution.py:78
  274.5 0.3 fusion.31
  274.8 0.4 convolution_subtract_fusion
  275.1 0.4 fusion.37
  275.5 11.1 %fusion.19 = f32[8192]{0:T(1024)S(1)} fusion(f32[8192,224]{1,0:T(8,128)} %bitcast.37, f32[96,224]{0,1:T(8,128)S(1)} %fusion.37, f32[128,224]{0,1:T(8,128)S(1)} %fusion.31), kind=kOutput, calls=%fused_computation.18 | convolution fusion | flops 4936213504 | bytes 7573504 | tf_op jit(solution)/shard_map/dot_general | solution.py:79
  286.6 0.1 div.39
  286.7 0.7 copy.17
  (19 shorter events, 0.2 us)
Async XLA Ops:
  6.5 173.8 %all-reduce.6.cloned.1.call-start = ((), (), s32[]{:S(2)}) async-start(), calls=%async_computation | async-start | bytes 458752 | tf_op jit(solution)/shard_map/psum | solution.py:54
  15.5 8.6 %collective-permute-start = (bf16[15,32,224]{2,1,0:T(8,128)(2,1)S(1)}, bf16[15,32,224]{2,1,0:T(8,128)(2,1)S(1)}, u32[]{:S(2)}, u32[]{:S(2)}) collective-permute-start(bf16[15,32,224]{2,1,0:T(8,128)(2,1)S(1)} %get-tuple-element.27), channel_id=1, source_target_pairs={{0,8},{8,16},{16,24},{1,9},{9,17},{17,25},{2,10},{10,18},{18,26},{... | collective-permute-start | bytes 645128 | tf_op jit(solution)/shard_map/ppermute | solution.py:15
  19.5 8.4 %collective-permute-start.1 = (bf16[15,32,224]{2,1,0:T(8,128)(2,1)S(1)}, bf16[15,32,224]{2,1,0:T(8,128)(2,1)S(1)}, u32[]{:S(2)}, u32[]{:S(2)}) collective-permute-start(bf16[15,32,224]{2,1,0:T(8,128)(2,1)S(1)} %get-tuple-element.28), channel_id=1, source_target_pairs={{8,0},{16,8},{24,16},{9,1},{17,9},{25,17},{10,2},{18,10},{26,18},{... | collective-permute-start | bytes 645128 | tf_op jit(solution)/shard_map/ppermute | solution.py:18
  32.5 29.1 %collective-permute-start.2 = (bf16[286,15,224]{2,0,1:T(8,128)(2,1)S(1)}, bf16[286,15,224]{2,0,1:T(8,128)(2,1)}, u32[]{:S(2)}, u32[]{:S(2)}) collective-permute-start(bf16[286,15,224]{2,0,1:T(8,128)(2,1)S(1)} %copy.9), channel_id=1, source_target_pairs={{0,1},{1,2},{2,3},{3,4},{4,5},{5,6},{6,7},{8,9},{9,10},{10,11},{11... | collective-permute-start | bytes 5765768 | tf_op jit(solution)/shard_map/ppermute | solution.py:15
  39.6 47.5 %collective-permute-start.3 = (bf16[286,15,224]{2,0,1:T(8,128)(2,1)}, bf16[286,15,224]{2,0,1:T(8,128)(2,1)}, u32[]{:S(2)}, u32[]{:S(2)}) collective-permute-start(bf16[286,15,224]{2,0,1:T(8,128)(2,1)} %copy.10), channel_id=1, source_target_pairs={{1,0},{2,1},{3,2},{4,3},{5,4},{6,5},{7,6},{9,8},{10,9},{11,10},{12... | collective-permute-start | bytes 5765768 | tf_op jit(solution)/shard_map/ppermute | solution.py:18
  41.5 48.4 %copy-start.1 = (bf16[256,32,224]{2,1,0:T(8,128)(2,1)S(1)}, bf16[256,32,224]{2,1,0:T(8,128)(2,1)}, u32[]{:S(2)}) copy-start(bf16[256,32,224]{2,1,0:T(8,128)(2,1)} %copy.6) | copy-start | bytes 11010052
  89.9 15.9 %copy-start.2 = (bf16[256,32,224]{0,2,1:T(8,128)(2,1)S(1)}, bf16[256,32,224]{0,2,1:T(8,128)(2,1)}, u32[]{:S(2)}) copy-start(bf16[256,32,224]{0,2,1:T(8,128)(2,1)} %param.1) | copy-start | bytes 11010052
  123.9 3.0 %copy-start = (f32[256,32,224]{0,2,1:T(8,128)}, f32[256,32,224]{0,2,1:T(8,128)S(1)}, u32[]{:S(2)}) copy-start(f32[256,32,224]{0,2,1:T(8,128)S(1)} %divide_subtract_fusion) | copy-start | bytes 22020100
  128.8 88.0 %all-reduce.8.cloned.1.call-start = ((), (), s32[]{:S(2)}) async-start(), calls=%async_computation.1 | async-start | bytes 458752 | tf_op jit(solution)/shard_map/psum | solution.py:55
Sparse Core Ops, SparseCore 0:
  128.9 51.4 all-reduce.5
  182.8 33.8 all-reduce.7
